TPU v7x, 512 devices: a whole 4x4x16 slice. The times are simulated.
512 devices in a mesh: grp: 16 (over z), wrk: 32 (over y, x, core).
Axes of the slice: x: 4, y: 4, z: 16, core: 2. Of those that a mesh axis runs over, the one named last changes fastest.
Arguments:
- orbitals: bfloat16 [512, 32, 1024], P(('grp', 'wrk')), may hold values from -6 to 6
- offsets: int32 [512, 3], replicated, may hold values from 0 to 135, as said below
- pair_slots: int32 [16, 32, 6, 2], P('grp', 'wrk'), may hold values from 0 to 511, as said below
- pair_count: int32 [16, 32], P('grp', 'wrk'), may hold values from 0 to 6, as said below
Outputs:
- exchange_fields: float32 [512, 32, 1024], P(('grp', 'wrk'))
Inputs may be any that keep to these rules, and one draw needn't show every extreme that they name: Row o gives the grid point of the first cell of orbital o's box; offsets of orbitals of the same or adjacent groups differ by less than 32 in each coordinate. Every slot of pair_slots[g, w] holds an orbital a of group g (numbers g * 32 to g * 32 + 31) and an orbital b other than a of group g or g + 1, with offsets of a and b differing by less than 32 in each coordinate; slots at or past pair_count[g, w] hold entries of the same kind that are not pairs. `pair_count`: the counts of every group sum to 96; in every group one worker has 6 pairs and one has none.
All inputs are finite; a program needn't handle non-finite values.
Results may differ from a plain program's by a relative error of at most 0.0003.
Values may be sent and summed in bfloat16 or wider, within the bound.
No kernel may reach another device: no remote copies, remote signals or barrier semaphores. Data moves between devices by JAX's collectives and lax.ppermute only.
A program may use at most 64 MiB of HBM per device.

v0:
```python
import jax
import jax.numpy as jnp
from jax import lax
from jax.sharding import PartitionSpec as P

screen_shift = 0.05
highest = lax.Precision.HIGHEST
EXCHANGE = "all_to_all"


def passed_along(value, axis, steps):
    count = lax.axis_size(axis)
    initial, last = (max(0, -steps), min(count, count - steps))
    return lax.ppermute(value, axis, [(source, source + steps) for source in range(initial, last)])


def sine_table(box_edge):
    counting = jnp.arange(box_edge, dtype=jnp.float32) + 1.0
    scaling = jnp.sqrt(2.0 / (box_edge + 1.0))
    return scaling * jnp.sin(jnp.pi * counting[:, None] * counting[None, :] / (box_edge + 1.0))


def inverse_symbol(box_edge):
    counting = jnp.arange(box_edge, dtype=jnp.float32) + 1.0
    eigen_one = 4.0 * jnp.sin(jnp.pi * counting / (2.0 * (box_edge + 1.0))) ** 2
    eigen_sum = eigen_one[:, None, None] + eigen_one[None, :, None] + eigen_one[None, None, :]
    return 1.0 / (eigen_sum + screen_shift)


def shift_matrices(offset_diff, box_edge):
    cell = jnp.arange(box_edge, dtype=jnp.int32)
    row_shift = cell[None, None, :] == cell[None, :, None] - offset_diff[:, 0, None, None]
    plane = jnp.arange(box_edge * box_edge, dtype=jnp.int32)
    out_y = (plane // box_edge)[None, :, None]
    out_z = (plane % box_edge)[None, :, None]
    in_y = (plane // box_edge)[None, None, :]
    in_z = (plane % box_edge)[None, None, :]
    plane_shift = (in_y == out_y - offset_diff[:, 1, None, None]) & (
        in_z == out_z - offset_diff[:, 2, None, None]
    )
    return (row_shift.astype(jnp.float32), plane_shift.astype(jnp.bfloat16))


def move_bf16(boxes, row_shift, plane_shift):
    planes = jnp.einsum("pxc,pyc->pxy", boxes, plane_shift, preferred_element_type=jnp.float32)
    return jnp.einsum("pxa,pac->pxc", row_shift, planes, precision=highest)


def unmove_f32(fields, row_shift, plane_shift):
    rows = jnp.einsum("pax,pac->pxc", row_shift, fields, precision=highest)
    high = lax.reduce_precision(rows, exponent_bits=8, mantissa_bits=7)
    rest = rows - high
    middle = lax.reduce_precision(rest, exponent_bits=8, mantissa_bits=7)
    low = rest - middle
    parts = jnp.concatenate([high, middle, low], axis=1).astype(jnp.bfloat16)
    moved = jnp.einsum("pxc,pcy->pxy", parts, plane_shift, preferred_element_type=jnp.float32)
    box_edge = fields.shape[1]
    return moved[:, :box_edge] + moved[:, box_edge : 2 * box_edge] + moved[:, 2 * box_edge :]


def solve_boxes(density, sine_rows, plane_sines, symbol):
    count_boxes, box_edge, plane_size = density.shape

    def apply_sines(field_block):
        along_first = jnp.einsum("kx,nxf->nkf", sine_rows, field_block, precision=highest)
        flat_rows = along_first.reshape(count_boxes * box_edge, plane_size)
        along_plane = jnp.dot(
            flat_rows, plane_sines, precision=highest, preferred_element_type=jnp.float32
        )
        return along_plane.reshape(count_boxes, box_edge, plane_size)

    spectrum = apply_sines(density) * symbol
    return apply_sines(spectrum)


def corner_of(orbital, offsets):
    listing = jnp.arange(offsets.shape[0], dtype=jnp.int32)
    chosen = orbital[:, None] == listing[None, :]
    return jnp.sum(jnp.where(chosen[:, :, None], offsets[None, :, :], 0), axis=1, dtype=jnp.int32)


def rows_to_orbitals(fields, rows, count):
    chosen = rows[:, None] == jnp.arange(count, dtype=jnp.int32)[None, :]
    return jnp.sum(jnp.where(chosen[:, :, None, None], fields[:, None, :, :], 0.0), axis=0)


def local(orbitals, offsets, pair_slots, pair_count):
    orb_dev, box_edge, plane_size = orbitals.shape
    workers = lax.axis_size("wrk")
    group_index = lax.axis_index("grp")
    grp_orbs = orb_dev * workers
    own_set = lax.all_gather(orbitals, "wrk", axis=0, tiled=True)
    upper_set = lax.all_gather(passed_along(orbitals, "grp", -1), "wrk", axis=0, tiled=True)
    group_set = jnp.concatenate([own_set, upper_set], axis=0)
    pair_list = pair_slots[0, 0]
    slot_cap = pair_list.shape[0]
    weights = (jnp.arange(slot_cap, dtype=jnp.int32) < pair_count[0, 0]).astype(jnp.float32)
    left_orb = pair_list[:, 0]
    right_orb = pair_list[:, 1]
    offset_diff = corner_of(right_orb, offsets) - corner_of(left_orb, offsets)
    base = group_index * grp_orbs
    left_row = jnp.clip(left_orb - base, 0, 2 * grp_orbs - 1)
    right_row = jnp.clip(right_orb - base, 0, 2 * grp_orbs - 1)
    left_boxes = jnp.take(group_set, left_row, axis=0)
    right_boxes = jnp.take(group_set, right_row, axis=0)
    row_shift, plane_shift = shift_matrices(offset_diff, box_edge)
    right_field = move_bf16(right_boxes, row_shift, plane_shift)
    sine_rows = sine_table(box_edge)
    plane_sines = (sine_rows[:, None, :, None] * sine_rows[None, :, None, :]).reshape(
        plane_size, plane_size
    )
    symbol = inverse_symbol(box_edge).reshape(box_edge, plane_size)
    left_field = left_boxes.astype(jnp.float32)
    potential = solve_boxes(left_field * right_field, sine_rows, plane_sines, symbol)
    weighted = potential * weights[:, None, None]
    to_left = weighted * right_field
    to_right = unmove_f32(weighted * left_field, row_shift, plane_shift)
    upper = right_row >= grp_orbs
    sent_fields = jnp.where(upper[:, None, None], to_right, 0.0)
    sent_rows = jnp.where(upper, right_row - grp_orbs, 0)
    got_fields = passed_along(sent_fields, "grp", 1)
    got_rows = passed_along(sent_rows, "grp", 1)
    kept_right = jnp.where(upper[:, None, None], 0.0, to_right)
    kept_rows = jnp.where(upper, 0, right_row)
    fields = jnp.concatenate([to_left, kept_right, got_fields], axis=0)
    rows = jnp.concatenate([left_row, kept_rows, got_rows], axis=0)
    combined = rows_to_orbitals(fields, rows, grp_orbs)
    if EXCHANGE == "all_to_all":
        pieces = lax.all_to_all(combined, "wrk", 0, 0, tiled=True)
        return jnp.sum(pieces, axis=0, keepdims=True)
    return lax.psum_scatter(combined, "wrk", scatter_dimension=0, tiled=True)


def solution(mesh):
    return jax.shard_map(
        local,
        mesh=mesh,
        in_specs=(P(("grp", "wrk"), None, None), P(), P("grp", "wrk", None, None), P("grp", "wrk")),
        out_specs=P(("grp", "wrk"), None, None),
        check_vma=False,
    )
```

profile of v0, /device:TPU:1, one launch (start us, length us, event | category | flops | bytes accessed | tf_op | source)
XLA Modules:
  0.0 274.2 jit_solution(15588823203964607802)
XLA Ops:
  6.5 0.0 all-gather.3.cloned.1.call-start
  6.5 0.7 all-gather.3.cloned.1.call-update
  7.3 0.0 all-gather.5.cloned.1.call-start
  7.3 1.3 collective-permute-start.1
  8.6 0.1 sine_multiply_fusion
  8.8 4.8 %collective-permute-done.1 = bf16[1,32,1024]{2,1,0:T(8,128)(2,1)S(1)} collective-permute-done((bf16[1,32,1024]{2,1,0:T(8,128)(2,1)}, bf16[1,32,1024]{2,1,0:T(8,128)(2,1)S(1)}, u32[]{:S(2)}, u32[]{:S(2)}) %collective-permute-start.1) | collective-permute-done | bytes 65568 | tf_op jit(solution)/shard_map/ppermute | solution.py:14
  13.5 0.6 copy-done.1
  14.2 0.0 all-gather.5.cloned.1.call-update
  14.2 8.0 %broadcast_multiply_fusion = f32[32,32,32,32]{3,2,1,0:T(8,128)} fusion(f32[32,32]{1,0:T(8,128)S(1)} %sine_multiply_fusion), kind=kLoop, calls=%fused_computation.14 | loop fusion | flops 1048576 | bytes 4198400 | tf_op jit(solution)/shard_map/mul | solution.py:109
  22.2 13.7 %reshape.409 = f32[1024,1024,1]{1,0,2:T(8,128)} reshape(f32[32,32,32,32]{3,2,1,0:T(8,128)} %broadcast_multiply_fusion) | data formatting | bytes 8388608 | tf_op jit(solution)/shard_map/mul | solution.py:109
  35.9 0.1 broadcast_add_fusion
  36.0 0.2 add.123
  36.2 0.2 add.124
  36.5 0.1 add.125
  37.2 0.0 copy-done.3
  37.2 0.1 iota_compare_fusion.3
  37.3 0.0 copy-done.2
  37.3 0.2 select_reduce_fusion.1
  37.6 0.1 iota_subtract_fusion
  37.7 0.1 broadcast_subtract_fusion
  37.8 0.1 broadcast_subtract_fusion.1
  37.9 37.2 %all-gather.3.cloned.1.call-done = bf16[32,32,1024]{2,1,0:T(8,128)(2,1)} async-done(((bf16[1,32,1024]{2,1,0:T(8,128)(2,1)}), bf16[32,32,1024]{2,1,0:T(8,128)(2,1)}) %all-gather.3.cloned.1.call-update) | async-done | bytes 2097168 | tf_op jit(solution)/shard_map/all_gather | solution.py:92
  75.1 3.2 %constant_dynamic-update-slice_fusion.1 = bf16[64,32,1024]{2,1,0:T(8,128)(2,1)} fusion(bf16[32,32,1024]{2,1,0:T(8,128)(2,1)} %all-gather.3.cloned.1.call-done), kind=kLoop, calls=%fused_computation.79 | loop fusion | bytes 4194304
  78.3 58.3 %all-gather.5.cloned.1.call-done = bf16[32,32,1024]{2,1,0:T(8,128)(2,1)} async-done(((bf16[1,32,1024]{2,1,0:T(8,128)(2,1)}), bf16[32,32,1024]{2,1,0:T(8,128)(2,1)}) %all-gather.5.cloned.1.call-update) | async-done | bytes 2097168 | tf_op jit(solution)/shard_map/all_gather | solution.py:93
  136.6 3.2 %constant_dynamic-update-slice_fusion = bf16[64,32,1024]{2,1,0:T(8,128)(2,1)} fusion(bf16[64,32,1024]{2,1,0:T(8,128)(2,1)} %constant_dynamic-update-slice_fusion.1, bf16[32,32,1024]{2,1,0:T(8,128)(2,1)} %all-gather.5.cloned.1.call-done), kind=kLoop, calls=%fused_computation.78 | loop fusion | bytes 4194304 | tf_op jit(solution)/shard_map/concatenate | solution.py:94
  139.8 2.8 %gather_fusion.1 = bf16[6,32,1024]{2,1,0:T(8,128)(2,1)S(1)} fusion(bf16[64,32,1024]{2,1,0:T(8,128)(2,1)} %constant_dynamic-update-slice_fusion, s32[1024]{0:T(1024)S(1)} %pad_clamp_fusion), kind=kCustom, calls=%fused_computation.1.clone | custom fusion | bytes 786456 | tf_op jit(solution)/shard_map/jit(_take)/gather | solution.py:105
  142.5 2.8 %gather_fusion = bf16[6,32,1024]{2,1,0:T(8,128)(2,1)S(1)} fusion(bf16[64,32,1024]{2,1,0:T(8,128)(2,1)} %constant_dynamic-update-slice_fusion, s32[1024]{0:T(1024)S(1)} %pad_clamp_fusion.1), kind=kCustom, calls=%fused_computation.clone | custom fusion | bytes 786456 | tf_op jit(solution)/shard_map/jit(_take)/gather | solution.py:104
  145.3 0.0 copy-start
  145.3 7.0 %fusion.1 = f32[6,32,1024]{2,1,0:T(8,128)S(1)} fusion(s32[6,1024]{1,0:T(8,128)S(1)} %broadcast_subtract_fusion, s32[1024]{0:T(1024)S(1)} %get-tuple-element.30, s32[6,1024]{1,0:T(8,128)S(1)} %broadcast_subtract_fusion.1, s32[1024]{0:T(1024)S(1)} %get-tuple-element.31, bf16[6,32,1024]{2,1,0:T(8,128)(2,1)S(1)} %gather_fusion.1, ...), kind=kOutput, calls=%fused_computation.5 | convolution fusion | flops 421724160 | bytes 1236998 | tf_op jit(solution)/shard_map/pxc,pyc->pxy/dot_general | solution.py:45
  152.3 0.5 fusion.20
  152.8 1.0 convolution_bitcast_fusion.1
  153.8 0.0 copy-done
  153.9 2.9 %convolution_multiply_fusion.1 = f32[6,32,1024]{2,1,0:T(8,128)S(1)} fusion(f32[6,32,1024]{2,1,0:T(8,128)S(1)} %convolution_bitcast_fusion.1, f32[1024,1024,1]{1,0,2:T(8,128)S(1)} %copy-done, f32[32,1024]{1,0:T(8,128)S(1)} %add_divide_fusion), kind=kOutput, calls=%fused_computation.19 | convolution fusion | flops 2416115712 | bytes 5898240 | tf_op jit(solution)/shard_map/dot_general | solution.py:67
  156.8 0.9 convolution_bitcast_fusion
  157.7 2.9 %fusion.48 = (f32[6,32,1024]{2,1,0:T(8,128)S(1)}, f32[6,32,1024]{2,1,0:T(8,128)S(1)}) fusion(f32[6,32,1024]{2,1,0:T(8,128)S(1)} %fusion.20, f32[6]{0:T(128)S(1)} %compare_convert_fusion, f32[6,32,1024]{2,1,0:T(8,128)S(1)} %convolution_bitcast_fusion, f32[1024,1024,1]{1,0,2:T(8,128)S(1)} %copy-done), kind=kOutput, calls=%fused_computation.108 | convolution fusion | flops 2416312320 | bytes 7340056 | tf_op jit(solution)/shard_map/dot_general | solution.py:67
  160.6 0.8 reduce-precision_convert_fusion.1
  161.5 7.1 %fusion = f32[6,96,1024]{2,1,0:T(8,128)S(1)} fusion(s32[6,1024]{1,0:T(8,128)S(1)} %broadcast_subtract_fusion, s32[1024]{0:T(1024)S(1)} %get-tuple-element.30, s32[6,1024]{1,0:T(8,128)S(1)} %broadcast_subtract_fusion.1, s32[1024]{0:T(1024)S(1)} %get-tuple-element.31, bf16[6,32,1024]{2,1,0:T(8,128)(2,1)S(1)} %get-tuple-element.15, ...), kind=kOutput, calls=%fused_computation.4 | convolution fusion | flops 1230372864 | bytes 3596288 | tf_op jit(solution)/shard_map/pxc,pcy->pxy/dot_general | solution.py:56
  168.6 0.3 broadcast_select_fusion.1
  168.8 3.2 %collective-permute-start.2 = (f32[6,32,1024]{2,1,0:T(8,128)S(1)}, f32[6,32,1024]{2,1,0:T(8,128)S(1)}, u32[]{:S(2)}, u32[]{:S(2)}) collective-permute-start(f32[6,32,1024]{2,1,0:T(8,128)S(1)} %get-tuple-element.13), channel_id=1, source_target_pairs={{0,32},{32,64},{64,96},{96,128},{128,160},{160,192},{192,224},{224... | collective-permute-start | bytes 2359304 | tf_op jit(solution)/shard_map/ppermute | solution.py:14
  172.1 3.1 %collective-permute-start = (s32[6]{0:T(128)S(1)}, s32[6]{0:T(128)S(1)}, u32[]{:S(2)}, u32[]{:S(2)}) collective-permute-start(s32[6]{0:T(128)S(1)} %get-tuple-element.22), channel_id=1, source_target_pairs={{0,32},{32,64},{64,96},{96,128},{128,160},{160,192},{192,224},{224... | collective-permute-start | bytes 80 | tf_op jit(solution)/shard_map/ppermute | solution.py:14
  175.2 13.4 %collective-permute-done = s32[6]{0:T(128)S(1)} collective-permute-done((s32[6]{0:T(128)S(1)}, s32[6]{0:T(128)S(1)}, u32[]{:S(2)}, u32[]{:S(2)}) %collective-permute-start) | collective-permute-done | bytes 56 | tf_op jit(solution)/shard_map/ppermute | solution.py:14
  188.7 0.1 pad_add_fusion
  188.7 0.1 iota_compare_fusion.5
  188.8 0.0 collective-permute-done.2
  188.8 0.3 pad_maximum_fusion
  189.1 18.2 %select_reduce_fusion = f32[32,32,1024]{2,1,0:T(8,128)} fusion(f32[18,32,1024]{2,1,0:T(8,128)S(1)} %pad_maximum_fusion, pred[18,32]{1,0:T(8,128)(4,1)S(1)} %iota_compare_fusion.5), kind=kLoop, calls=%fused_computation.2 | loop fusion | flops 36700160 | bytes 6554176 | tf_op jit(solution)/shard_map/reduce_sum | solution.py:84
  207.3 57.0 %all_to_all.5 = f32[32,32,1024]{2,1,0:T(8,128)} all-to-all(f32[32,32,1024]{2,1,0:T(8,128)} %select_reduce_fusion), channel_id=1, replica_groups=mesh['grp'=16,'wrk'=32] {'wrk'}, dimensions={0} | all-to-all | bytes 8388608 | tf_op jit(solution)/shard_map/all_to_all | solution.py:129
  264.3 3.1 %reduce_sum.39 = f32[32,1024]{1,0:T(8,128)} reduce(f32[32,32,1024]{2,1,0:T(8,128)} %all_to_all.5, f32[]{:T(128)} %constant.85.clone.1), dimensions={0}, to_apply=%region_3.5 | reduce | flops 1015808 | bytes 4325380 | tf_op jit(solution)/shard_map/reduce_sum | solution.py:130
  (19 shorter events, 0.2 us)
Async XLA Ops:
  6.5 68.6 %all-gather.3.cloned.1.call-start = ((), (), s32[]{:S(2)}) async-start(), calls=%async_computation.1 | async-start | bytes 2162688 | tf_op jit(solution)/shard_map/all_gather | solution.py:92
  7.3 129.3 %all-gather.5.cloned.1.call-start = ((), (), s32[]{:S(2)}) async-start(), calls=%async_computation.2 | async-start | bytes 2162688 | tf_op jit(solution)/shard_map/all_gather | solution.py:93
  7.3 6.2 %collective-permute-start.1 = (bf16[1,32,1024]{2,1,0:T(8,128)(2,1)}, bf16[1,32,1024]{2,1,0:T(8,128)(2,1)S(1)}, u32[]{:S(2)}, u32[]{:S(2)}) collective-permute-start(bf16[1,32,1024]{2,1,0:T(8,128)(2,1)} %param.6), channel_id=1, source_target_pairs={{32,0},{64,32},{96,64},{128,96},{160,128},{192,160},{224,192},{256... | collective-permute-start | bytes 196616 | tf_op jit(solution)/shard_map/ppermute | solution.py:14
  13.5 0.6 copy-start.1
  22.2 15.0 %copy-start.3 = (s32[1,1,6,2]{2,3,1,0:T(2,128)S(1)}, s32[1,1,6,2]{2,3,1,0:T(2,128)}, u32[]{:S(2)}) copy-start(s32[1,1,6,2]{2,3,1,0:T(2,128)} %param.8) | copy-start | bytes 148
  22.2 15.1 %copy-start.2 = (s32[512,3]{0,1:T(4,128)S(1)}, s32[512,3]{0,1:T(4,128)}, u32[]{:S(2)}) copy-start(s32[512,3]{0,1:T(4,128)} %param.7) | copy-start | bytes 18436
  145.3 8.6 %copy-start = (f32[1024,1024,1]{1,0,2:T(8,128)S(1)}, f32[1024,1024,1]{1,0,2:T(8,128)}, u32[]{:S(2)}) copy-start(f32[1024,1024,1]{1,0,2:T(8,128)} %reshape.409) | copy-start | bytes 12582916
  168.8 20.0 %collective-permute-start.2 = (f32[6,32,1024]{2,1,0:T(8,128)S(1)}, f32[6,32,1024]{2,1,0:T(8,128)S(1)}, u32[]{:S(2)}, u32[]{:S(2)}) collective-permute-start(f32[6,32,1024]{2,1,0:T(8,128)S(1)} %get-tuple-element.13), channel_id=1, source_target_pairs={{0,32},{32,64},{64,96},{96,128},{128,160},{160,192},{192,224},{224... | collective-permute-start | bytes 2359304 | tf_op jit(solution)/shard_map/ppermute | solution.py:14
  172.1 16.6 %collective-permute-start = (s32[6]{0:T(128)S(1)}, s32[6]{0:T(128)S(1)}, u32[]{:S(2)}, u32[]{:S(2)}) collective-permute-start(s32[6]{0:T(128)S(1)} %get-tuple-element.22), channel_id=1, source_target_pairs={{0,32},{32,64},{64,96},{96,128},{128,160},{160,192},{192,224},{224... | collective-permute-start | bytes 80 | tf_op jit(solution)/shard_map/ppermute | solution.py:14
Sparse Core Ops, SparseCore 0:
  10.5 64.5 all-gather.2
  78.2 58.3 all-gather.4
where the time goes:
time: 275 us; the launch traced here: 274 us
  waiting for transfers between devices  114 us (41%)
  blocking collectives  57 us (21%)
  other arithmetic  30.8 us (11%)
  local copies, waits for them, and re-layouts  26.8 us (10%)
  matrix products  23.2 us (8%)
  between operations  14.3 us (5%)
  starting transfers between devices  7.69 us (3%)
    all_gather x1, waiting for transfers between devices, local(): lax.all_gather(passed_along(orbitals, 'grp', -1), 'wrk', axis=0, tiled=True)  58.3 us
    all_to_all x1, blocking collectives, local(): pieces = lax.all_to_all(combined, 'wrk', 0, 0, tiled=True)  57 us
    all_gather x1, waiting for transfers between devices, local(): own_set = lax.all_gather(orbitals, 'wrk', axis=0, tiled=True)  37.2 us
    reduce_sum x1, other arithmetic, rows_to_orbitals(): jnp.sum(jnp.where(chosen[:, :, None, None], fields[:, None, :, :], 0.0),...  18.2 us
    ppermute x3, waiting for transfers between devices, passed_along(): lax.ppermute(value, axis, [(source, source + steps) for source in range(i...  18.2 us
    mul x1, local copies, waits for them, and re-layouts, local(): sine_rows[:, None, :, None] * sine_rows[None, :, None, :]  13.7 us
    mul x1, other arithmetic, local(): sine_rows[:, None, :, None] * sine_rows[None, :, None, :]  8 us
    ppermute x3, starting transfers between devices, passed_along(): lax.ppermute(value, axis, [(source, source + steps) for source in range(i...  7.65 us
  transfers between devices with their start and end apart: 5, of which 4 were waited for; matrix products, arithmetic and copies ran while one was open for 10% of the time, Pallas kernels for 0%

commit v1 on v0

--- a/solution.py
+++ b/solution.py
@@ -89,7 +89,9 @@
     workers = lax.axis_size("wrk")
     group_index = lax.axis_index("grp")
     grp_orbs = orb_dev * workers
-    own_set = lax.all_gather(orbitals, "wrk", axis=0, tiled=True)
+    own_set = jnp.concatenate(
+        lax.all_to_all(jnp.stack([orbitals] * lax.axis_size("wrk")), "wrk", 0, 0), axis=0
+    )
     upper_set = lax.all_gather(passed_along(orbitals, "grp", -1), "wrk", axis=0, tiled=True)
     group_set = jnp.concatenate([own_set, upper_set], axis=0)
     pair_list = pair_slots[0, 0]

time: 275 us -> 227 us (0.83)
  waiting for transfers between devices: 114 us -> 55.8 us
  starting transfers between devices: 7.69 us -> 18.3 us
  local copies, waits for them, and re-layouts: 26.8 us -> 22.8 us
  other arithmetic: 30.8 us -> 34.7 us
    all_gather x1 -> x0, waiting for transfers between devices: 37.2 us -> none  [local(): own_set = lax.all_gather(orbitals, 'wrk', axis=0, tiled=True)]
    all_gather x1, waiting for transfers between devices: 58.3 us -> 38.5 us  [local(): lax.all_gather(passed_along(orbitals, 'grp', -1), 'wrk', axis=0, tiled=True)]
    all_to_all x0 -> x1, starting transfers between devices: none -> 10.5 us  [local(): lax.all_to_all(jnp.stack([orbitals] * lax.axis_size('wrk')), 'wrk', 0, 0)]
    ppermute x3, waiting for transfers between devices: 18.2 us -> 13.4 us  [passed_along(): lax.ppermute(value, axis, [(source, source + steps) for source in range(i...]
    concatenate x0 -> x1, other arithmetic: none -> 3.9 us  [local(): group_set = jnp.concatenate([own_set, upper_set], axis=0)]
    all_to_all x0 -> x1, waiting for transfers between devices: none -> 3.81 us  [local(): lax.all_to_all(jnp.stack([orbitals] * lax.axis_size('wrk')), 'wrk', 0, 0)]
    unnamed x9 -> x8, local copies, waits for them, and re-layouts: 3.85 us -> 0.64 us
    concatenate x1 -> x0, local copies, waits for them, and re-layouts: 3.19 us -> none  [local(): group_set = jnp.concatenate([own_set, upper_set], axis=0)]
  transfers between devices with their start and end apart: 5 -> 5, of which waited for: 4 -> 3; matrix products, arithmetic and copies ran while one was open for 10% -> 11% of each run, Pallas kernels for 0% -> 0%
where the time goes in v1:
time: 227 us; the launch traced here: 226 us
  blocking collectives  57 us (25%)
  waiting for transfers between devices  55.8 us (25%)
  other arithmetic  34.7 us (15%)
  matrix products  23.1 us (10%)
  local copies, waits for them, and re-layouts  22.8 us (10%)
  starting transfers between devices  18.3 us (8%)
  between operations  14.3 us (6%)
    all_to_all x1, blocking collectives, local(): pieces = lax.all_to_all(combined, 'wrk', 0, 0, tiled=True)  57 us
    all_gather x1, waiting for transfers between devices, local(): lax.all_gather(passed_along(orbitals, 'grp', -1), 'wrk', axis=0, tiled=True)  38.5 us
    reduce_sum x1, other arithmetic, rows_to_orbitals(): jnp.sum(jnp.where(chosen[:, :, None, None], fields[:, None, :, :], 0.0),...  18.2 us
    mul x1, local copies, waits for them, and re-layouts, local(): sine_rows[:, None, :, None] * sine_rows[None, :, None, :]  13.7 us
    ppermute x3, waiting for transfers between devices, passed_along(): lax.ppermute(value, axis, [(source, source + steps) for source in range(i...  13.4 us
    all_to_all x1, starting transfers between devices, local(): lax.all_to_all(jnp.stack([orbitals] * lax.axis_size('wrk')), 'wrk', 0, 0)  10.5 us
    mul x1, other arithmetic, local(): sine_rows[:, None, :, None] * sine_rows[None, :, None, :]  7.99 us
    ppermute x3, starting transfers between devices, passed_along(): lax.ppermute(value, axis, [(source, source + steps) for source in range(i...  7.78 us
  transfers between devices with their start and end apart: 5, of which 3 were waited for; matrix products, arithmetic and copies ran while one was open for 11% of the time, Pallas kernels for 0%

profile of v1, /device:TPU:1, one launch (start us, length us, event | category | flops | bytes accessed | tf_op | source)
XLA Modules:
  0.0 226.0 jit_solution(15299299111658692111)
XLA Ops:
  6.5 1.4 collective-permute-start.1
  8.0 2.4 %stack.2 = bf16[32,1,32,1024]{3,2,1,0:T(8,128)(2,1)} broadcast(bf16[32,1024]{1,0:T(8,128)(2,1)} %bitcast.40), dimensions={2,3} | broadcast | bytes 2162688 | tf_op jit(solution)/shard_map/stack | solution.py:93
  10.4 10.5 %all-to-all-start = ((bf16[32,1,32,1024]{3,2,1,0:T(8,128)(2,1)}), bf16[32,1,32,1024]{3,2,1,0:T(8,128)(2,1)S(1)}, u32[]{:S(2)}, u32[]{:S(2)}) async-start(bf16[32,1,32,1024]{3,2,1,0:T(8,128)(2,1)} %stack.2), calls=%async_computation | async-start | bytes 4194304 | tf_op jit(solution)/shard_map/all_to_all | solution.py:93
  20.9 0.0 all-gather.2.cloned.1.call-start
  21.0 0.0 copy-done.3
  21.0 0.0 collective-permute-done.1
  21.1 0.0 copy-start.1
  21.1 0.6 copy-done.1
  21.7 0.0 all-gather.2.cloned.1.call-update
  22.4 0.1 iota_compare_fusion.3
  22.5 0.0 copy-done.2
  22.5 0.2 select_reduce_fusion.1
  22.7 0.1 broadcast_add_fusion
  22.8 0.1 sine_multiply_fusion
  22.9 8.0 %broadcast_multiply_fusion = f32[32,32,32,32]{3,2,1,0:T(8,128)} fusion(f32[32,32]{1,0:T(8,128)S(1)} %sine_multiply_fusion), kind=kLoop, calls=%fused_computation.14 | loop fusion | flops 1048576 | bytes 4198400 | tf_op jit(solution)/shard_map/mul | solution.py:111
  30.9 13.7 %reshape.416 = f32[1024,1024,1]{1,0,2:T(8,128)} reshape(f32[32,32,32,32]{3,2,1,0:T(8,128)} %broadcast_multiply_fusion) | data formatting | bytes 8388608 | tf_op jit(solution)/shard_map/mul | solution.py:111
  44.6 0.2 add.123
  44.8 0.2 add.124
  45.0 0.1 add.125
  45.2 0.1 iota_subtract_fusion
  45.2 0.1 broadcast_subtract_fusion
  45.3 0.1 broadcast_subtract_fusion.1
  45.4 3.8 %all-to-all-done = bf16[32,1,32,1024]{3,2,1,0:T(8,128)(2,1)S(1)} async-done(((bf16[32,1,32,1024]{3,2,1,0:T(8,128)(2,1)}), bf16[32,1,32,1024]{3,2,1,0:T(8,128)(2,1)S(1)}, u32[]{:S(2)}, u32[]{:S(2)}) %all-to-all-start) | async-done | bytes 2097184 | tf_op jit(solution)/shard_map/all_to_all | solution.py:93
  49.2 38.5 %all-gather.2.cloned.1.call-done = bf16[32,32,1024]{2,1,0:T(8,128)(2,1)} async-done(((bf16[1,32,1024]{2,1,0:T(8,128)(2,1)}), bf16[32,32,1024]{2,1,0:T(8,128)(2,1)}) %all-gather.2.cloned.1.call-update) | async-done | bytes 2097168 | tf_op jit(solution)/shard_map/all_gather | solution.py:95
  87.7 3.9 %pad_maximum_fusion = bf16[64,32,1024]{2,1,0:T(8,128)(2,1)} fusion(bf16[32,32,1024]{2,1,0:T(8,128)(2,1)} %all-gather.2.cloned.1.call-done, bf16[32,32,1024]{2,1,0:T(8,128)(2,1)S(1)} %bitcast.39), kind=kLoop, calls=%fused_computation.15 | loop fusion | flops 2097152 | bytes 8388608 | tf_op jit(solution)/shard_map/concatenate | solution.py:96
  91.6 2.8 %gather_fusion.1 = bf16[6,32,1024]{2,1,0:T(8,128)(2,1)S(1)} fusion(bf16[64,32,1024]{2,1,0:T(8,128)(2,1)} %pad_maximum_fusion, s32[1024]{0:T(1024)S(1)} %pad_clamp_fusion), kind=kCustom, calls=%fused_computation.1.clone | custom fusion | bytes 786456 | tf_op jit(solution)/shard_map/jit(_take)/gather | solution.py:107
  94.4 2.8 %gather_fusion = bf16[6,32,1024]{2,1,0:T(8,128)(2,1)S(1)} fusion(bf16[64,32,1024]{2,1,0:T(8,128)(2,1)} %pad_maximum_fusion, s32[1024]{0:T(1024)S(1)} %pad_clamp_fusion.1), kind=kCustom, calls=%fused_computation.clone | custom fusion | bytes 786456 | tf_op jit(solution)/shard_map/jit(_take)/gather | solution.py:106
  97.2 0.0 copy-start
  97.2 7.0 %fusion.1 = f32[6,32,1024]{2,1,0:T(8,128)S(1)} fusion(s32[6,1024]{1,0:T(8,128)S(1)} %broadcast_subtract_fusion, s32[1024]{0:T(1024)S(1)} %get-tuple-element.30, s32[6,1024]{1,0:T(8,128)S(1)} %broadcast_subtract_fusion.1, s32[1024]{0:T(1024)S(1)} %get-tuple-element.31, bf16[6,32,1024]{2,1,0:T(8,128)(2,1)S(1)} %gather_fusion.1, ...), kind=kOutput, calls=%fused_computation.5 | convolution fusion | flops 421724160 | bytes 1236998 | tf_op jit(solution)/shard_map/pxc,pyc->pxy/dot_general | solution.py:45
  104.2 0.5 fusion.20
  104.7 1.0 convolution_bitcast_fusion.1
  105.7 0.0 copy-done
  105.7 2.9 %convolution_multiply_fusion.1 = f32[6,32,1024]{2,1,0:T(8,128)S(1)} fusion(f32[6,32,1024]{2,1,0:T(8,128)S(1)} %convolution_bitcast_fusion.1, f32[1024,1024,1]{1,0,2:T(8,128)S(1)} %copy-done, f32[32,1024]{1,0:T(8,128)S(1)} %add_divide_fusion), kind=kOutput, calls=%fused_computation.20 | convolution fusion | flops 2416115712 | bytes 5898240 | tf_op jit(solution)/shard_map/dot_general | solution.py:67
  108.6 0.9 convolution_bitcast_fusion
  109.6 2.9 %fusion.48 = (f32[6,32,1024]{2,1,0:T(8,128)S(1)}, f32[6,32,1024]{2,1,0:T(8,128)S(1)}) fusion(f32[6,32,1024]{2,1,0:T(8,128)S(1)} %fusion.20, f32[6]{0:T(128)S(1)} %compare_convert_fusion, f32[6,32,1024]{2,1,0:T(8,128)S(1)} %convolution_bitcast_fusion, f32[1024,1024,1]{1,0,2:T(8,128)S(1)} %copy-done), kind=kOutput, calls=%fused_computation.107 | convolution fusion | flops 2416312320 | bytes 7340056 | tf_op jit(solution)/shard_map/dot_general | solution.py:67
  112.5 0.8 reduce-precision_convert_fusion.1
  113.3 7.1 %fusion = f32[6,96,1024]{2,1,0:T(8,128)S(1)} fusion(s32[6,1024]{1,0:T(8,128)S(1)} %broadcast_subtract_fusion, s32[1024]{0:T(1024)S(1)} %get-tuple-element.30, s32[6,1024]{1,0:T(8,128)S(1)} %broadcast_subtract_fusion.1, s32[1024]{0:T(1024)S(1)} %get-tuple-element.31, bf16[6,32,1024]{2,1,0:T(8,128)(2,1)S(1)} %get-tuple-element.15, ...), kind=kOutput, calls=%fused_computation.4 | convolution fusion | flops 1230372864 | bytes 3596288 | tf_op jit(solution)/shard_map/pxc,pcy->pxy/dot_general | solution.py:56
  120.4 0.3 broadcast_select_fusion.1
  120.7 3.2 %collective-permute-start.2 = (f32[6,32,1024]{2,1,0:T(8,128)S(1)}, f32[6,32,1024]{2,1,0:T(8,128)S(1)}, u32[]{:S(2)}, u32[]{:S(2)}) collective-permute-start(f32[6,32,1024]{2,1,0:T(8,128)S(1)} %get-tuple-element.13), channel_id=1, source_target_pairs={{0,32},{32,64},{64,96},{96,128},{128,160},{160,192},{192,224},{224... | collective-permute-start | bytes 2359304 | tf_op jit(solution)/shard_map/ppermute | solution.py:14
  123.9 3.1 %collective-permute-start = (s32[6]{0:T(128)S(1)}, s32[6]{0:T(128)S(1)}, u32[]{:S(2)}, u32[]{:S(2)}) collective-permute-start(s32[6]{0:T(128)S(1)} %get-tuple-element.22), channel_id=1, source_target_pairs={{0,32},{32,64},{64,96},{96,128},{128,160},{160,192},{192,224},{224... | collective-permute-start | bytes 80 | tf_op jit(solution)/shard_map/ppermute | solution.py:14
  127.0 13.4 %collective-permute-done = s32[6]{0:T(128)S(1)} collective-permute-done((s32[6]{0:T(128)S(1)}, s32[6]{0:T(128)S(1)}, u32[]{:S(2)}, u32[]{:S(2)}) %collective-permute-start) | collective-permute-done | bytes 56 | tf_op jit(solution)/shard_map/ppermute | solution.py:14
  140.5 0.1 pad_add_fusion
  140.6 0.1 iota_compare_fusion.5
  140.6 0.0 collective-permute-done.2
  140.6 0.2 pad_maximum_fusion.1
  140.9 18.2 %select_reduce_fusion = f32[32,32,1024]{2,1,0:T(8,128)} fusion(f32[18,32,1024]{2,1,0:T(8,128)S(1)} %pad_maximum_fusion.1, pred[18,32]{1,0:T(8,128)(4,1)S(1)} %iota_compare_fusion.5), kind=kLoop, calls=%fused_computation.2 | loop fusion | flops 36700160 | bytes 6554176 | tf_op jit(solution)/shard_map/reduce_sum | solution.py:84
  159.1 57.0 %all_to_all.10 = f32[32,32,1024]{2,1,0:T(8,128)} all-to-all(f32[32,32,1024]{2,1,0:T(8,128)} %select_reduce_fusion), channel_id=1, replica_groups=mesh['grp'=16,'wrk'=32] {'wrk'}, dimensions={0} | all-to-all | bytes 8388608 | tf_op jit(solution)/shard_map/all_to_all | solution.py:131
  216.1 3.1 %reduce_sum.39 = f32[32,1024]{1,0:T(8,128)} reduce(f32[32,32,1024]{2,1,0:T(8,128)} %all_to_all.10, f32[]{:T(128)} %constant.85.clone.1), dimensions={0}, to_apply=%region_3.5 | reduce | flops 1015808 | bytes 4325380 | tf_op jit(solution)/shard_map/reduce_sum | solution.py:132
  (18 shorter events, 0.2 us)
Async XLA Ops:
  6.5 14.4 %copy-start.3 = (s32[1,1,6,2]{2,3,1,0:T(2,128)S(1)}, s32[1,1,6,2]{2,3,1,0:T(2,128)}, u32[]{:S(2)}) copy-start(s32[1,1,6,2]{2,3,1,0:T(2,128)} %param.8) | copy-start | bytes 148
  6.5 16.0 %copy-start.2 = (s32[512,3]{0,1:T(4,128)S(1)}, s32[512,3]{0,1:T(4,128)}, u32[]{:S(2)}) copy-start(s32[512,3]{0,1:T(4,128)} %param.7) | copy-start | bytes 18436
  6.5 14.5 %collective-permute-start.1 = (bf16[1,32,1024]{2,1,0:T(8,128)(2,1)}, bf16[1,32,1024]{2,1,0:T(8,128)(2,1)S(1)}, u32[]{:S(2)}, u32[]{:S(2)}) collective-permute-start(bf16[1,32,1024]{2,1,0:T(8,128)(2,1)} %param.6), channel_id=1, source_target_pairs={{32,0},{64,32},{96,64},{128,96},{160,128},{192,160},{224,192},{256... | collective-permute-start | bytes 196616 | tf_op jit(solution)/shard_map/ppermute | solution.py:14
  10.4 38.8 %all-to-all-start = ((bf16[32,1,32,1024]{3,2,1,0:T(8,128)(2,1)}), bf16[32,1,32,1024]{3,2,1,0:T(8,128)(2,1)S(1)}, u32[]{:S(2)}, u32[]{:S(2)}) async-start(bf16[32,1,32,1024]{3,2,1,0:T(8,128)(2,1)} %stack.2), calls=%async_computation | async-start | bytes 4194304 | tf_op jit(solution)/shard_map/all_to_all | solution.py:93
  20.9 66.8 %all-gather.2.cloned.1.call-start = ((), (), s32[]{:S(2)}) async-start(), calls=%async_computation.2 | async-start | bytes 2162688 | tf_op jit(solution)/shard_map/all_gather | solution.py:95
  21.1 0.6 copy-start.1
  97.2 8.5 %copy-start = (f32[1024,1024,1]{1,0,2:T(8,128)S(1)}, f32[1024,1024,1]{1,0,2:T(8,128)}, u32[]{:S(2)}) copy-start(f32[1024,1024,1]{1,0,2:T(8,128)} %reshape.416) | copy-start | bytes 12582916
  120.7 20.0 %collective-permute-start.2 = (f32[6,32,1024]{2,1,0:T(8,128)S(1)}, f32[6,32,1024]{2,1,0:T(8,128)S(1)}, u32[]{:S(2)}, u32[]{:S(2)}) collective-permute-start(f32[6,32,1024]{2,1,0:T(8,128)S(1)} %get-tuple-element.13), channel_id=1, source_target_pairs={{0,32},{32,64},{64,96},{96,128},{128,160},{160,192},{192,224},{224... | collective-permute-start | bytes 2359304 | tf_op jit(solution)/shard_map/ppermute | solution.py:14
  123.9 16.6 %collective-permute-start = (s32[6]{0:T(128)S(1)}, s32[6]{0:T(128)S(1)}, u32[]{:S(2)}, u32[]{:S(2)}) collective-permute-start(s32[6]{0:T(128)S(1)} %get-tuple-element.22), channel_id=1, source_target_pairs={{0,32},{32,64},{64,96},{96,128},{128,160},{160,192},{192,224},{224... | collective-permute-start | bytes 80 | tf_op jit(solution)/shard_map/ppermute | solution.py:14
Sparse Core Ops, SparseCore 0:
  24.9 62.8 all-gather.1
